TPU v7x, 256 devices: a whole 4x4x8 slice. The times are simulated.
256 devices in a mesh: gx: 32 (over y, z_hi, core), gz: 8 (over z_lo, x).
Axes of the slice: x: 4, y: 4, z: 8 (z_hi: 4, z_lo: 2; z = z_hi * 2 + z_lo), core: 2. Of those that a mesh axis runs over, the one named last changes fastest.
Arguments:
- scalars: float32 [2, 4096, 128, 256], P(None, 'gx', 'gz'), may hold values from -6 to 6
- diffusivity: float32 [4096, 128, 256], P('gx', 'gz'), may hold values from 0.01 to 0.1
- reaction_rate: float32 [4096, 128, 256], P('gx', 'gz'), may hold values from 0.05 to 1
- block_inverse: float32 [2, 32, 128, 128], P(None, 'gx'), may hold values from 0 to 1
- block_response: float32 [2, 32, 128], P(None, 'gx'), may hold values from 0 to 1, as said below
- mean_profile: float32 [2, 256], replicated, may hold values from -4 to 4
- recycle_gain: float32 [2, 256], replicated, may hold values from 0.5 to 1.5
- station_index: int32 [1], replicated, may hold values from 0 to 4095
- span_shift: int32 [1], replicated, may hold values from 0 to 127
Outputs:
- transported: float32 [2, 4096, 128, 256], P(None, 'gx', 'gz')
Inputs may be any that keep to these rules, and one draw needn't show every extreme that they name: `block_response`: every entry is positive.
All inputs are finite; a program needn't handle non-finite values.
Results may differ from a plain program's by a relative error of at most 0.0003.
Values sent between devices are 32-bit elements; how exact they have to be, the bound alone decides.
No kernel may reach another device: no remote copies, remote signals or barrier semaphores. Data moves between devices by JAX's collectives and lax.ppermute only.
A program may use at most 64 MiB of HBM per device.

v0:
```python
import jax
import jax.numpy as jnp
from jax import lax
from jax.sharding import PartitionSpec as P

reaction_yields = (-1.0, 1.0)


def from_root(x, axis, root):
    mine = lax.axis_index(axis) == root
    return lax.psum(jnp.where(mine, x, jnp.zeros_like(x)), axis)


def with_halo(x, sides, width, wrap):
    for axis, dim in sides:
        devices, length = (lax.axis_size(axis), x.shape[dim])
        up = [(i, (i + 1) % devices) for i in range(devices if wrap else devices - 1)]
        down = [(j, i) for i, j in up]
        last = lax.slice_in_dim(x, length - width, length, axis=dim)
        first = lax.slice_in_dim(x, 0, width, axis=dim)
        before = lax.ppermute(last, axis, up)
        after = lax.ppermute(first, axis, down)
        x = jnp.concatenate([before, x, after], axis=dim)
    return x


def prefix(part, axis, combine, identity):
    place = lax.axis_index(axis)
    gathered = jax.tree.map(lambda a: lax.all_gather(a, axis), part)
    state = jax.tree.map(lambda a, e: jnp.zeros_like(a) + jnp.asarray(e, a.dtype), part, identity)

    def one(hop, state):
        return combine(
            state, jax.tree.map(lambda a: lax.dynamic_index_in_dim(a, hop, 0, False), gathered)
        )

    return lax.fori_loop(0, place, one, state)


def fourth_order(padded, dimension, length):

    def shifted(offset):
        return lax.slice_in_dim(padded, offset, offset + length, axis=dimension)

    return (
        -shifted(0) + 16.0 * shifted(1) - 30.0 * shifted(2) + 16.0 * shifted(3) - shifted(4)
    ) / 12.0


def make_inflow(station_plane, mean_profile, recycle_gain, span_shift):
    span_mean = jnp.mean(station_plane, axis=1, keepdims=True)
    rolled = jnp.roll(station_plane, span_shift[0], axis=1)
    return mean_profile[:, None, :] + recycle_gain[:, None, :] * (rolled - span_mean)


def explicit_part(stream_padded, span_padded, center, diffusivity, reaction_rate):
    wall_padded = jnp.pad(center, ((0, 0), (0, 0), (0, 0), (2, 2)))
    laplacian = fourth_order(stream_padded, 1, center.shape[1])
    laplacian = laplacian + fourth_order(span_padded, 2, center.shape[2])
    laplacian = laplacian + fourth_order(wall_padded, 3, center.shape[3])
    reaction = reaction_rate * jax.nn.softplus(center[0]) * jax.nn.softplus(center[1])
    source = jnp.stack([reaction_yields[0] * reaction, reaction_yields[1] * reaction])
    return center + diffusivity[None] * laplacian + source


def on_device(
    scalars,
    diffusivity,
    reaction_rate,
    block_inverse,
    block_response,
    mean_profile,
    recycle_gain,
    station_index,
    span_shift,
):
    plane_count = scalars.shape[1]
    span_cells = scalars.shape[2]
    stream_devices = lax.axis_size("gx")
    stream_rank = lax.axis_index("gx")
    span_rank = lax.axis_index("gz")
    owner_row = station_index[0] // plane_count
    local_plane = station_index[0] - owner_row * plane_count
    own_slice = lax.dynamic_index_in_dim(scalars, local_plane, 1, keepdims=False)
    arrived = from_root(own_slice, "gx", owner_row)
    station_plane = lax.all_gather(arrived, "gz", axis=1, tiled=True)
    inflow_full = make_inflow(station_plane, mean_profile, recycle_gain, span_shift)
    inflow = lax.dynamic_slice_in_dim(inflow_full, span_rank * span_cells, span_cells, 1)
    stream_padded = with_halo(scalars, (("gx", 1),), 2, False)
    edge_shape = (scalars.shape[0], 2, scalars.shape[2], scalars.shape[3])
    inlet_planes = jnp.broadcast_to(inflow[:, None], edge_shape)
    outlet_planes = jnp.broadcast_to(scalars[:, -1:], edge_shape)
    head_planes = jnp.where(stream_rank == 0, inlet_planes, stream_padded[:, :2])
    tail_planes = jnp.where(stream_rank == stream_devices - 1, outlet_planes, stream_padded[:, -2:])
    window = jnp.concatenate([head_planes, stream_padded[:, 2:-2], tail_planes], axis=1)
    span_padded = with_halo(scalars, (("gz", 2),), 2, True)
    explicit = explicit_part(window, span_padded, scalars, diffusivity, reaction_rate)
    local_part = jnp.einsum(
        "sij,sjzy->sizy", block_inverse[:, 0], explicit, precision=lax.Precision.HIGHEST
    )
    response = block_response[:, 0]
    exit_plane = local_part[:, -1]
    exit_ratio = response[:, -1]

    def compose(earlier_part, later_part):
        return (
            earlier_part[0] * later_part[0],
            later_part[0][:, None, None] * earlier_part[1] + later_part[1],
        )

    identity = (jnp.ones_like(exit_ratio), jnp.zeros_like(exit_plane))
    through, upstream_sum = prefix((exit_ratio, exit_plane), "gx", compose, identity)
    incoming = through[:, None, None] * inflow + upstream_sum
    return local_part + response[:, :, None, None] * incoming[:, None]


def solution(mesh):
    return jax.shard_map(
        on_device,
        mesh=mesh,
        in_specs=(
            P(None, "gx", "gz", None),
            P("gx", "gz", None),
            P("gx", "gz", None),
            P(None, "gx", None, None),
            P(None, "gx", None),
            P(),
            P(),
            P(),
            P(),
        ),
        out_specs=P(None, "gx", "gz", None),
        check_vma=False,
    )
```

profile of v0, /device:TPU:217, one launch (start us, length us, event | category | flops | bytes accessed | tf_op | source)
XLA Modules:
  0.0 334.0 jit_solution(15417572126514026074)
XLA Ops:
  6.5 1.6 fusion.48
  8.1 1.3 collective-permute-start
  9.4 3.8 %collective-permute-start.1 = (f32[2,2,16,256]{3,2,1,0:T(8,128)}, f32[2,2,16,256]{3,2,1,0:T(8,128)}, u32[]{:S(2)}, u32[]{:S(2)}) collective-permute-start(f32[2,2,16,256]{3,2,1,0:T(8,128)} %get-tuple-element.62), channel_id=1, source_target_pairs={{8,0},{16,8},{24,16},{32,24},{40,32},{48,40},{56,48},{64,56},{72,6... | collective-permute-start | bytes 196616 | tf_op jit(solution)/shard_map/ppermute | solution.py:22
  13.3 3.6 %fusion.47 = (f32[2,128,2,256]{3,2,1,0:T(2,128)}, f32[2,128,2,256]{3,2,1,0:T(2,128)}) fusion(f32[2,128,16,256]{3,2,1,0:T(8,128)} %param.11), kind=kLoop, calls=%fused_computation.82 | loop fusion | bytes 2097152 | tf_op jit(solution)/shard_map/slice | solution.py:20
  16.9 2.9 collective-permute-start.3
  21.1 1.4 slice_bitcast_fusion
  22.5 0.9 slice_reduce_fusion
  24.2 1.3 dynamic-slice
  26.3 137.6 %all-reduce.2 = (f32[2,16,256]{2,1,0:T(8,128)S(1)}, f32[64]{0:T(128)S(1)}) all-reduce(f32[2,16,256]{2,1,0:T(8,128)S(1)} %fusion.44, f32[64]{0:T(128)S(1)} %dynamic-update-slice), channel_id=1, replica_groups=mesh['gx'=32,'gz'=8] {'gx'}, use_global_device_ids=true, to_apply=%region_0.1 | all-reduce | flops 8256 | bytes 66048 | tf_op jit(solution)/shard_map/psum | solution.py:11
  163.9 22.5 %all_gather.9 = f32[2,128,256]{2,1,0:T(8,128)S(1)} all-gather(f32[2,16,256]{2,1,0:T(8,128)S(1)} %get-tuple-element.53), channel_id=1, replica_groups=mesh['gx'=32,'gz'=8] {'gz'}, dimensions={1}, use_global_device_ids=true | all-gather | bytes 294912 | tf_op jit(solution)/shard_map/all_gather | solution.py:86
  186.5 6.7 %multiply_bitcast_fusion = (f32[1,128,16,256]{3,2,1,0:T(8,128)S(1)}, f32[128,16,256]{2,1,0:T(8,128)}) fusion(f32[2,128,16,256]{3,2,1,0:T(8,128)} %param.11, f32[128,16,256]{2,1,0:T(8,128)} %param.13), kind=kLoop, calls=%fused_computation.64 | loop fusion | flops 7864320 | bytes 10485760 | tf_op jit(solution)/shard_map/stack | solution.py:62
  193.1 1.6 broadcast_multiply_fusion
  195.4 4.7 %constant_dynamic-update-slice_fusion.1 = f32[2,128,18,256]{3,2,1,0:T(8,128)} fusion(f32[2,128,16,256]{3,2,1,0:T(8,128)} %param.11), kind=kLoop, calls=%fused_computation.78 | loop fusion | bytes 8388608
  200.0 0.9 broadcast_select_fusion.1
  201.7 1.1 constant_dynamic-update-slice_fusion
  202.7 25.1 %fusion.8 = f32[2,128,16,256]{3,2,1,0:T(8,128)S(1)} fusion(f32[2,128,16,256]{3,2,1,0:T(8,128)} %param.11, f32[2,2,16,256]{3,2,1,0:T(8,128)S(1)} %broadcast_select_fusion, f32[2,2,16,256]{3,2,1,0:T(8,128)S(1)} %broadcast_select_fusion.1, f32[2,128,2,256]{3,2,1,0:T(2,128)S(1)} %collective-permute-done.2, ...), kind=kLoop, calls=%fused_computation.22 | loop fusion | flops 35651584 | bytes 23724032 | tf_op jit(solution)/shard_map/add | solution.py:63
  227.8 6.3 %fusion.29 = f32[2,128,16,256]{3,1,2,0:T(8,128)S(1)} fusion(f32[2,128,16,256]{3,2,1,0:T(8,128)S(1)} %fusion.8, f32[2,1,128,128]{3,2,1,0:T(8,128)S(1)} %copy-done), kind=kOutput, calls=%fused_computation.49 | convolution fusion | flops 1610612736 | bytes 8519680 | tf_op jit(solution)/shard_map/sij,sjzy->sizy/dot_general | solution.py:98
  234.2 2.0 copy-done.1
  237.0 56.6 %all-gather.4.cloned.1.call-done = f32[64,1,16,256]{3,2,1,0:T(8,128)} async-done(((f32[2,1,16,256]{3,2,1,0:T(8,128)}), f32[64,1,16,256]{3,2,1,0:T(8,128)}) %all-gather.4.cloned.1.call-update) | async-done | bytes 1048592 | tf_op jit(solution)/shard_map/all_gather | solution.py:29
  293.6 26.3 %while.12 = (s32[]{:T(128)}, f32[2]{0:T(128)S(1)}, f32[2,16,256]{2,1,0:T(8,128)S(1)}, s32[]{:T(128)}, f32[32,2]{1,0:T(8,128)S(1)}, /*index=5*/f32[32,2,16,256]{3,2,1,0:T(8,128)}, s32[]{:T(128)}, s32[]{:T(128)}, s32[]{:T(128)}) while((s32[]{:T(128)}, f32[2]{0:T(128)S(1)}, f32[2,16,256]{2,1,0:T(8,128)S(1)}, s32[]{:T(128)}, ...), condition=%wide.region_3.4_spmd, body=%wide.region_2.3_spmd.sunk | while | flops 16391 | bytes 98479 | solution.py:37
  294.5 0.8 bitcast_add_fusion.2
  295.3 0.8 bitcast_add_fusion.2
  296.2 0.8 bitcast_add_fusion.2
  297.0 0.8 bitcast_add_fusion.2
  297.9 0.8 bitcast_add_fusion.2
  298.7 0.8 bitcast_add_fusion.2
  299.6 0.8 bitcast_add_fusion.2
  300.4 0.8 bitcast_add_fusion.2
  301.3 0.8 bitcast_add_fusion.2
  302.1 0.8 bitcast_add_fusion.2
  302.9 0.8 bitcast_add_fusion.2
  303.8 0.8 bitcast_add_fusion.2
  304.6 0.8 bitcast_add_fusion.2
  305.5 0.8 bitcast_add_fusion.2
  306.3 0.8 bitcast_add_fusion.2
  307.2 0.8 bitcast_add_fusion.2
  308.0 0.8 bitcast_add_fusion.2
  308.9 0.8 bitcast_add_fusion.2
  309.7 0.8 bitcast_add_fusion.2
  310.6 0.8 bitcast_add_fusion.2
  311.4 0.8 bitcast_add_fusion.2
  313.1 0.8 bitcast_add_fusion.2
  314.0 0.8 bitcast_add_fusion.2
  315.7 0.8 bitcast_add_fusion.2
  316.5 0.8 bitcast_add_fusion.2
  319.1 0.8 bitcast_add_fusion.2
  320.0 2.7 multiply_add_fusion
  322.7 4.4 %copy.19 = f32[2,128,16,256]{3,2,1,0:T(8,128)} copy(f32[2,128,16,256]{3,1,2,0:T(8,128)S(1)} %multiply_add_fusion) | data formatting | bytes 8388608 | tf_op jit(solution)/shard_map/add | solution.py:114
  (67 shorter events, 7.9 us)
Async XLA Ops:
  6.5 221.3 %copy-start = (f32[2,1,128,128]{3,2,1,0:T(8,128)S(1)}, f32[2,1,128,128]{3,2,1,0:T(8,128)}, u32[]{:S(2)}) copy-start(f32[2,1,128,128]{3,2,1,0:T(8,128)} %param.14) | copy-start | bytes 393220
  6.5 287.1 %all-gather.4.cloned.1.call-start = ((), (), s32[]{:S(2)}) async-start(), calls=%async_computation | async-start | bytes 1081344 | tf_op jit(solution)/shard_map/all_gather | solution.py:29
  8.1 191.9 %collective-permute-start = (f32[2,2,16,256]{3,2,1,0:T(8,128)}, f32[2,2,16,256]{3,2,1,0:T(8,128)}, u32[]{:S(2)}, u32[]{:S(2)}) collective-permute-start(f32[2,2,16,256]{3,2,1,0:T(8,128)} %get-tuple-element.61), channel_id=1, source_target_pairs={{0,8},{8,16},{16,24},{24,32},{32,40},{40,48},{48,56},{56,64},{64,7... | collective-permute-start | bytes 196616 | tf_op jit(solution)/shard_map/ppermute | solution.py:21
  9.4 191.5 %collective-permute-start.1 = (f32[2,2,16,256]{3,2,1,0:T(8,128)}, f32[2,2,16,256]{3,2,1,0:T(8,128)}, u32[]{:S(2)}, u32[]{:S(2)}) collective-permute-start(f32[2,2,16,256]{3,2,1,0:T(8,128)} %get-tuple-element.62), channel_id=1, source_target_pairs={{8,0},{16,8},{24,16},{32,24},{40,32},{48,40},{56,48},{64,56},{72,6... | collective-permute-start | bytes 196616 | tf_op jit(solution)/shard_map/ppermute | solution.py:22
  16.9 184.8 %collective-permute-start.3 = (f32[2,128,2,256]{3,2,1,0:T(2,128)}, f32[2,128,2,256]{3,2,1,0:T(2,128)S(1)}, u32[]{:S(2)}, u32[]{:S(2)}) collective-permute-start(f32[2,128,2,256]{3,2,1,0:T(2,128)} %get-tuple-element.59), channel_id=1, source_target_pairs={{1,0},{2,1},{3,2},{4,3},{5,4},{6,5},{7,6},{0,7},{9,8},{10,9},{11,1... | collective-permute-start | bytes 1572872 | tf_op jit(solution)/shard_map/ppermute | solution.py:22
  19.8 182.9 %collective-permute-start.2 = (f32[2,128,2,256]{3,2,1,0:T(2,128)}, f32[2,128,2,256]{3,2,1,0:T(2,128)S(1)}, u32[]{:S(2)}, u32[]{:S(2)}) collective-permute-start(f32[2,128,2,256]{3,2,1,0:T(2,128)} %get-tuple-element.60), channel_id=1, source_target_pairs={{0,1},{1,2},{2,3},{3,4},{4,5},{5,6},{6,7},{7,0},{8,9},{9,10},{10,1... | collective-permute-start | bytes 1572872 | tf_op jit(solution)/shard_map/ppermute | solution.py:21
  186.4 6.7 %copy-start.2 = (f32[128,16,256]{2,1,0:T(8,128)S(1)}, f32[128,16,256]{2,1,0:T(8,128)}, u32[]{:S(2)}) copy-start(f32[128,16,256]{2,1,0:T(8,128)} %param.12) | copy-start | bytes 6291460
  193.1 1.6 copy-start.3
  193.1 1.6 copy-start.4
  227.8 92.1 %copy-start.5 = (f32[2,1,128]{2,1,0:T(1,128)S(1)}, f32[2,1,128]{2,1,0:T(1,128)}, u32[]{:S(2)}) copy-start(f32[2,1,128]{2,1,0:T(1,128)} %param.15) | copy-start | bytes 3076
  234.2 2.0 copy-start.1
Sparse Core Ops, SparseCore 0:
  237.0 56.5 all-gather.3
where the time goes:
time: 337 us; the launch traced here: 334 us
  blocking collectives  160 us (47%)
  other arithmetic  65.5 us (19%)
  waiting for transfers between devices  56.6 us (17%)
  local copies, waits for them, and re-layouts  21.9 us (6%)
  between operations  15.5 us (5%)
  starting transfers between devices  8.06 us (2%)
  matrix products  6.35 us (2%)
    psum x1, blocking collectives, from_root(): return lax.psum(jnp.where(mine, x, jnp.zeros_like(x)), axis)  138 us
    all_gather x1, waiting for transfers between devices, prefix(): gathered = jax.tree.map(lambda a: lax.all_gather(a, axis), part)  56.6 us
    add x31, other arithmetic, compose(): later_part[0][:, None, None] * earlier_part[1] + later_part[1]  25.9 us
    add x1, other arithmetic, explicit_part(): return center + diffusivity[None] * laplacian + source  25.1 us
    all_gather x1, blocking collectives, on_device(): station_plane = lax.all_gather(arrived, 'gz', axis=1, tiled=True)  22.5 us
    unnamed x16, local copies, waits for them, and re-layouts  8.19 us
    ppermute x2, starting transfers between devices, with_halo(): after = lax.ppermute(first, axis, down)  6.77 us
  transfers between devices with their start and end apart: 5, of which 1 were waited for; matrix products, arithmetic and copies ran while one was open for 7% of the time, Pallas kernels for 0%

commit v1 on v0

--- a/solution.py
+++ b/solution.py
@@ -7,8 +7,14 @@
 
 
 def from_root(x, axis, root):
+
+    def _fit_ways(raw, a_name):
+        all_values = lax.all_gather(raw, a_name)
+        seen_now = jnp.sum(all_values, axis=0)
+        return seen_now
+
     mine = lax.axis_index(axis) == root
-    return lax.psum(jnp.where(mine, x, jnp.zeros_like(x)), axis)
+    return _fit_ways(jnp.where(mine, x, jnp.zeros_like(x)), a_name=axis)
 
 
 def with_halo(x, sides, width, wrap):

time: 337 us -> 235 us (0.70)
  blocking collectives: 160 us -> 93.8 us
  waiting for transfers between devices: 56.6 us -> 24.6 us
  local copies, waits for them, and re-layouts: 21.9 us -> 18.2 us
    psum x1 -> x0, blocking collectives: 138 us -> none  [from_root(): return lax.psum(jnp.where(mine, x, jnp.zeros_like(x)), axis)]
    unnamed x0 -> x1, blocking collectives: none -> 71.3 us
    all_gather x1, waiting for transfers between devices: 56.6 us -> 0.02 us  [prefix(): gathered = jax.tree.map(lambda a: lax.all_gather(a, axis), part)]
    all_gather x0 -> x1, waiting for transfers between devices: none -> 24.5 us  [_fit_ways(): all_values = lax.all_gather(raw, a_name)]
    unnamed x16 -> x20, local copies, waits for them, and re-layouts: 8.19 us -> 6.73 us
  transfers between devices with their start and end apart: 5 -> 6, of which waited for: 1 -> 1; matrix products, arithmetic and copies ran while one was open for 7% -> 9% of each run, Pallas kernels for 0% -> 0%
where the time goes in v1:
time: 235 us; the launch traced here: 233 us
  blocking collectives  93.8 us (40%)
  other arithmetic  66.5 us (28%)
  waiting for transfers between devices  24.6 us (10%)
  local copies, waits for them, and re-layouts  18.2 us (8%)
  between operations  15.6 us (7%)
  starting transfers between devices  7.47 us (3%)
  matrix products  6.35 us (3%)
    unnamed x1, blocking collectives  71.3 us
    add x31, other arithmetic, compose(): later_part[0][:, None, None] * earlier_part[1] + later_part[1]  25.9 us
    add x1, other arithmetic, explicit_part(): return center + diffusivity[None] * laplacian + source  24.9 us
    all_gather x1, waiting for transfers between devices, _fit_ways(): all_values = lax.all_gather(raw, a_name)  24.5 us
    all_gather x1, blocking collectives, on_device(): station_plane = lax.all_gather(arrived, 'gz', axis=1, tiled=True)  22.5 us
    unnamed x20, local copies, waits for them, and re-layouts  6.73 us
    another operation x1, other arithmetic, explicit_part(): jnp.stack([reaction_yields[0] * reaction, reaction_yields[1] * reaction])  6.72 us
    dot_general x1, matrix products, on_device(): jnp.einsum('sij,sjzy->sizy', block_inverse[:, 0], explicit, precision=lax...  6.35 us
  transfers between devices with their start and end apart: 6, of which 1 were waited for; matrix products, arithmetic and copies ran while one was open for 9% of the time, Pallas kernels for 0%

profile of v1, /device:TPU:217, one launch (start us, length us, event | category | flops | bytes accessed | tf_op | source)
XLA Modules:
  0.0 232.6 jit_solution(1179631154448709611)
XLA Ops:
  7.3 1.4 dynamic-slice_select_fusion
  8.7 1.5 fusion.47
  10.2 1.3 collective-permute-start
  11.5 3.2 %collective-permute-start.1 = (f32[2,2,16,256]{3,2,1,0:T(8,128)S(1)}, f32[2,2,16,256]{3,2,1,0:T(8,128)S(1)}, u32[]{:S(2)}, u32[]{:S(2)}) collective-permute-start(f32[2,2,16,256]{3,2,1,0:T(8,128)S(1)} %get-tuple-element.62), channel_id=1, source_target_pairs={{8,0},{16,8},{24,16},{32,24},{40,32},{48,40},{56,48},{64,56},{72,6... | collective-permute-start | bytes 196616 | tf_op jit(solution)/shard_map/ppermute | solution.py:28
  14.8 3.6 %fusion.46 = (f32[2,128,2,256]{3,2,1,0:T(2,128)}, f32[2,128,2,256]{3,2,1,0:T(2,128)}) fusion(f32[2,128,16,256]{3,2,1,0:T(8,128)} %param.11), kind=kLoop, calls=%fused_computation.82 | loop fusion | bytes 2097152 | tf_op jit(solution)/shard_map/slice | solution.py:26
  18.3 2.9 %collective-permute-start.3 = (f32[2,128,2,256]{3,2,1,0:T(2,128)}, f32[2,128,2,256]{3,2,1,0:T(2,128)S(1)}, u32[]{:S(2)}, u32[]{:S(2)}) collective-permute-start(f32[2,128,2,256]{3,2,1,0:T(2,128)} %get-tuple-element.57), channel_id=1, source_target_pairs={{1,0},{2,1},{3,2},{4,3},{5,4},{6,5},{7,6},{0,7},{9,8},{10,9},{11,1... | collective-permute-start | bytes 1572872 | tf_op jit(solution)/shard_map/ppermute | solution.py:28
  21.2 6.7 %multiply_bitcast_fusion = (f32[1,128,16,256]{3,2,1,0:T(8,128)S(1)}, f32[128,16,256]{2,1,0:T(8,128)}) fusion(f32[2,128,16,256]{3,2,1,0:T(8,128)} %param.11, f32[128,16,256]{2,1,0:T(8,128)} %param.13), kind=kLoop, calls=%fused_computation.64 | loop fusion | flops 7864320 | bytes 10485760 | tf_op jit(solution)/shard_map/stack | solution.py:68
  28.0 1.6 broadcast_multiply_fusion
  29.6 1.4 copy-done.1
  30.9 2.5 %constant_dynamic-update-slice_fusion.1 = f32[2,128,18,256]{3,2,1,0:T(8,128)} fusion(f32[2,128,16,256]{3,2,1,0:T(8,128)S(1)} %copy-done.1), kind=kLoop, calls=%fused_computation.78 | loop fusion | bytes 8388608
  34.7 1.0 constant_dynamic-update-slice_fusion
  35.7 24.5 %all-gather.6.cloned.1.call-done = f32[64,1,16,256]{3,2,1,0:T(8,128)} async-done(((f32[2,1,16,256]{3,2,1,0:T(8,128)}), f32[64,1,16,256]{3,2,1,0:T(8,128)}) %all-gather.6.cloned.1.call-update) | async-done | bytes 1048592 | tf_op jit(solution)/shard_map/all_gather | solution.py:12
  60.3 1.3 bitcast_reduce_fusion
  61.5 22.5 %all_gather.14 = f32[2,128,256]{2,1,0:T(8,128)S(1)} all-gather(f32[2,16,256]{2,1,0:T(8,128)S(1)} %bitcast_reduce_fusion), channel_id=1, replica_groups=mesh['gx'=32,'gz'=8] {'gz'}, dimensions={1}, use_global_device_ids=true | all-gather | bytes 294912 | tf_op jit(solution)/shard_map/all_gather | solution.py:92
  84.2 0.9 broadcast_select_fusion.1
  85.1 24.9 %fusion.8 = f32[2,128,16,256]{3,2,1,0:T(8,128)S(1)} fusion(f32[2,128,16,256]{3,2,1,0:T(8,128)} %param.11, f32[2,2,16,256]{3,2,1,0:T(8,128)} %broadcast_select_fusion, f32[2,2,16,256]{3,2,1,0:T(8,128)S(1)} %broadcast_select_fusion.1, f32[2,128,2,256]{3,2,1,0:T(2,128)S(1)} %collective-permute-done.2, f32[2,128,18,256]{3,2,1,0:T(8,128)} %constant_dynamic-update-slice_fusion, ...), kind=kLoop, calls=%fused_computation.22 | loop fusion | flops 35651584 | bytes 23724032 | tf_op jit(solution)/shard_map/add | solution.py:69
  110.0 6.3 %fusion.29 = f32[2,128,16,256]{3,1,2,0:T(8,128)S(1)} fusion(f32[2,128,16,256]{3,2,1,0:T(8,128)S(1)} %fusion.8, f32[2,1,128,128]{3,2,1,0:T(8,128)S(1)} %copy-done), kind=kOutput, calls=%fused_computation.49 | convolution fusion | flops 1610612736 | bytes 8519680 | tf_op jit(solution)/shard_map/sij,sjzy->sizy/dot_general | solution.py:104
  116.3 2.0 copy-done.2
  120.7 71.3 %all-reduce.1 = f32[64]{0:T(128)S(1)} all-reduce(f32[64]{0:T(128)S(1)} %dynamic-update-slice), channel_id=3, replica_groups=mesh['gx'=32,'gz'=8] {'gx'}, use_global_device_ids=true, to_apply=%add.1 | all-reduce | flops 64 | bytes 512
  192.2 26.3 %while.12 = (s32[]{:T(128)}, f32[2]{0:T(128)S(1)}, f32[2,16,256]{2,1,0:T(8,128)S(1)}, s32[]{:T(128)}, f32[32,2]{1,0:T(8,128)S(1)}, /*index=5*/f32[32,2,16,256]{3,2,1,0:T(8,128)}, s32[]{:T(128)}, s32[]{:T(128)}, s32[]{:T(128)}) while((s32[]{:T(128)}, f32[2]{0:T(128)S(1)}, f32[2,16,256]{2,1,0:T(8,128)S(1)}, s32[]{:T(128)}, ...), condition=%wide.region_3.4_spmd, body=%wide.region_2.3_spmd.sunk | while | flops 16391 | bytes 98479 | solution.py:43
  192.3 0.8 bitcast_add_fusion.2
  193.1 0.8 bitcast_add_fusion.2
  194.0 0.8 bitcast_add_fusion.2
  194.8 0.8 bitcast_add_fusion.2
  195.6 0.8 bitcast_add_fusion.2
  196.5 0.8 bitcast_add_fusion.2
  197.3 0.8 bitcast_add_fusion.2
  198.2 0.8 bitcast_add_fusion.2
  199.0 0.8 bitcast_add_fusion.2
  199.9 0.8 bitcast_add_fusion.2
  200.7 0.8 bitcast_add_fusion.2
  201.6 0.8 bitcast_add_fusion.2
  202.4 0.8 bitcast_add_fusion.2
  203.3 0.8 bitcast_add_fusion.2
  204.1 0.8 bitcast_add_fusion.2
  205.0 0.8 bitcast_add_fusion.2
  205.8 0.8 bitcast_add_fusion.2
  206.7 0.8 bitcast_add_fusion.2
  207.5 0.8 bitcast_add_fusion.2
  208.4 0.8 bitcast_add_fusion.2
  209.2 0.8 bitcast_add_fusion.2
  210.9 0.8 bitcast_add_fusion.2
  211.8 0.8 bitcast_add_fusion.2
  214.3 0.8 bitcast_add_fusion.2
  215.1 0.8 bitcast_add_fusion.2
  217.7 0.8 bitcast_add_fusion.2
  218.6 2.7 %multiply_add_fusion = f32[2,128,16,256]{3,1,2,0:T(8,128)S(1)} fusion(f32[2,128,16,256]{3,1,2,0:T(8,128)} %copy-done.2, f32[2,16,256]{2,1,0:T(8,128)S(1)} %multiply_add_fusion.1, f32[2,128]{1,0:T(2,128)S(1)} %bitcast.74), kind=kLoop, calls=%fused_computation.48 | loop fusion | flops 2097152 | bytes 8422400 | tf_op jit(solution)/shard_map/add | solution.py:120
  221.4 4.4 %copy.16 = f32[2,128,16,256]{3,2,1,0:T(8,128)} copy(f32[2,128,16,256]{3,1,2,0:T(8,128)S(1)} %multiply_add_fusion) | data formatting | bytes 8388608 | tf_op jit(solution)/shard_map/add | solution.py:120
  (74 shorter events, 7.3 us)
Async XLA Ops:
  6.5 103.4 %copy-start = (f32[2,1,128,128]{3,2,1,0:T(8,128)S(1)}, f32[2,1,128,128]{3,2,1,0:T(8,128)}, u32[]{:S(2)}) copy-start(f32[2,1,128,128]{3,2,1,0:T(8,128)} %param.14) | copy-start | bytes 393220
  6.5 53.7 %all-gather.6.cloned.1.call-start = ((), (), s32[]{:S(2)}) async-start(), calls=%async_computation | async-start | bytes 1081344 | tf_op jit(solution)/shard_map/all_gather | solution.py:12
  8.7 183.5 %all-gather.8.cloned.1.call-start = ((), (), s32[]{:S(2)}) async-start(), calls=%async_computation.1 | async-start | bytes 1081344 | tf_op jit(solution)/shard_map/all_gather | solution.py:35
  10.2 73.9 %collective-permute-start = (f32[2,2,16,256]{3,2,1,0:T(8,128)}, f32[2,2,16,256]{3,2,1,0:T(8,128)}, u32[]{:S(2)}, u32[]{:S(2)}) collective-permute-start(f32[2,2,16,256]{3,2,1,0:T(8,128)} %get-tuple-element.61), channel_id=1, source_target_pairs={{0,8},{8,16},{16,24},{24,32},{32,40},{40,48},{48,56},{56,64},{64,7... | collective-permute-start | bytes 196616 | tf_op jit(solution)/shard_map/ppermute | solution.py:27
  11.5 22.5 %collective-permute-start.1 = (f32[2,2,16,256]{3,2,1,0:T(8,128)S(1)}, f32[2,2,16,256]{3,2,1,0:T(8,128)S(1)}, u32[]{:S(2)}, u32[]{:S(2)}) collective-permute-start(f32[2,2,16,256]{3,2,1,0:T(8,128)S(1)} %get-tuple-element.62), channel_id=1, source_target_pairs={{8,0},{16,8},{24,16},{32,24},{40,32},{48,40},{56,48},{64,56},{72,6... | collective-permute-start | bytes 196616 | tf_op jit(solution)/shard_map/ppermute | solution.py:28
  18.3 16.4 %collective-permute-start.3 = (f32[2,128,2,256]{3,2,1,0:T(2,128)}, f32[2,128,2,256]{3,2,1,0:T(2,128)S(1)}, u32[]{:S(2)}, u32[]{:S(2)}) collective-permute-start(f32[2,128,2,256]{3,2,1,0:T(2,128)} %get-tuple-element.57), channel_id=1, source_target_pairs={{1,0},{2,1},{3,2},{4,3},{5,4},{6,5},{7,6},{0,7},{9,8},{10,9},{11,1... | collective-permute-start | bytes 1572872 | tf_op jit(solution)/shard_map/ppermute | solution.py:28
  21.2 6.7 %copy-start.3 = (f32[128,16,256]{2,1,0:T(8,128)S(1)}, f32[128,16,256]{2,1,0:T(8,128)}, u32[]{:S(2)}) copy-start(f32[128,16,256]{2,1,0:T(8,128)} %param.12) | copy-start | bytes 6291460
  21.2 63.8 %collective-permute-start.2 = (f32[2,128,2,256]{3,2,1,0:T(2,128)}, f32[2,128,2,256]{3,2,1,0:T(2,128)S(1)}, u32[]{:S(2)}, u32[]{:S(2)}) collective-permute-start(f32[2,128,2,256]{3,2,1,0:T(2,128)} %get-tuple-element.58), channel_id=1, source_target_pairs={{0,1},{1,2},{2,3},{3,4},{4,5},{5,6},{6,7},{7,0},{8,9},{9,10},{10,1... | collective-permute-start | bytes 1572872 | tf_op jit(solution)/shard_map/ppermute | solution.py:27
  28.0 3.0 %copy-start.1 = (f32[2,128,16,256]{3,2,1,0:T(8,128)S(1)}, f32[2,128,16,256]{3,2,1,0:T(8,128)}, u32[]{:S(2)}) copy-start(f32[2,128,16,256]{3,2,1,0:T(8,128)} %param.11) | copy-start | bytes 12582916
  30.9 53.2 %copy-start.4 = (f32[2,256]{1,0:T(2,128)S(1)}, f32[2,256]{1,0:T(2,128)}, u32[]{:S(2)}) copy-start(f32[2,256]{1,0:T(2,128)} %param.16) | copy-start | bytes 6148
  30.9 53.2 %copy-start.5 = (f32[2,256]{1,0:T(2,128)S(1)}, f32[2,256]{1,0:T(2,128)}, u32[]{:S(2)}) copy-start(f32[2,256]{1,0:T(2,128)} %param.17) | copy-start | bytes 6148
  110.0 9.1 %copy-start.7 = (u32[256]{0:T(256)S(1)}, u32[256]{0:T(256)}, u32[]{:S(2)}) copy-start(u32[256]{0:T(256)} %constant.95) | copy-start | bytes 3076
  110.0 10.3 %copy-start.6 = (f32[2,1,128]{2,1,0:T(1,128)S(1)}, f32[2,1,128]{2,1,0:T(1,128)}, u32[]{:S(2)}) copy-start(f32[2,1,128]{2,1,0:T(1,128)} %param.15) | copy-start | bytes 3076
  116.3 2.0 copy-start.2
Sparse Core Ops, SparseCore 0:
  9.9 50.2 all-gather.5
  119.1 55.4 all-gather.7
